TPU v7x, 256 devices: a whole 4x4x8 slice. The times are simulated.
256 devices in a mesh: req: 32 (over x, y, core), tp: 8 (over z).
Axes of the slice: x: 4, y: 4, z: 8, core: 2. Of those that a mesh axis runs over, the one named last changes fastest.
Arguments:
- query: bfloat16 [768, 4096], P('req', 'tp'), may hold values from -102 to 102
- new_key: bfloat16 [768, 1024], P('req', 'tp'), may hold values from -6 to 6
- new_value: bfloat16 [768, 1024], P('req', 'tp'), may hold values from -6 to 6
- prefix_key: bfloat16 [64, 6144, 1024], P('req', None, 'tp'), may hold values from -6 to 6
- prefix_value: bfloat16 [64, 6144, 1024], P('req', None, 'tp'), may hold values from -6 to 6
- suffix_key: bfloat16 [768, 128, 1024], P('req', None, 'tp'), may hold values from -6 to 6
- suffix_value: bfloat16 [768, 128, 1024], P('req', None, 'tp'), may hold values from -6 to 6
- group_ids: int32 [768], replicated, may hold values from 0 to 63, as said below
- prompt_len: int32 [64], P('req'), may hold values from 768 to 6144, as said below
- suffix_len: int32 [768], replicated, may hold values from 1 to 128, as said below
- o_weight: bfloat16 [4096, 4096], P('tp'), may hold values from -0.09375 to 0.09375
- residual: bfloat16 [768, 4096], P('req'), may hold values from -0.29882812 to 0.29882812
- norm_gain: bfloat16 [4096], replicated, may hold values from 0.5 to 1.5
Outputs:
- hidden: bfloat16 [768, 4096], P('req')
- normed: bfloat16 [768, 4096], P('req')
Inputs may be any that keep to these rules, and one draw needn't show every extreme that they name: Request r belongs to group group_ids[r]; groups 2k to 2k + 1 at a time are held together (group // 2 names the holder). Among each aligned block of 24 requests, every holder that appears is named by exactly 2 of them. `prompt_len`: some group has exactly 6144. `suffix_len`: some request has exactly 128.
All inputs are finite; a program needn't handle non-finite values.
Results may differ from a plain program's by a relative error of at most 0.008.
Values may be sent and summed in bfloat16 or wider, within the bound.
No kernel may reach another device: no remote copies, remote signals or barrier semaphores. Data moves between devices by JAX's collectives and lax.ppermute only.
A program may use at most 64 MiB of HBM per device.

v0:
```python
import math
import jax
import jax.numpy as jnp
from jax import lax
from jax.sharding import PartitionSpec as P

HD = 128
WIN = 4096
SINKS = 4
FAR_BELOW = -1e30
NORM_EPS = 1e-06


def prefix_attend(
    rows_query, row_group, row_suffix, prefix_key, prefix_value, prompt_len, first_group, blocks
):
    row_count = rows_query.shape[0]
    groups_dev = prefix_key.shape[0]
    prompt_max = prefix_key.shape[1]
    kv_dev = prefix_key.shape[2] // HD
    heads_dev = rows_query.shape[1] // HD
    repeat = heads_dev // kv_dev
    block_len = min(512, prompt_max)
    score_scale = 1.0 / math.sqrt(HD)
    local_group = row_group - first_group
    owned = (local_group >= 0) & (local_group < groups_dev)
    member = local_group[:, None] == jnp.arange(groups_dev, dtype=jnp.int32)[None, :]
    row_prompt = jnp.sum(jnp.where(member, prompt_len[None, :], 0), axis=1)
    row_low = row_prompt + row_suffix - WIN + 1
    queries = rows_query.reshape(row_count, kv_dev, repeat, HD)

    def key_step(block_index, loop_state):
        running, weight_sum, weighted = loop_state
        key_start = block_index * block_len
        key_block = lax.dynamic_slice_in_dim(prefix_key, key_start, block_len, 1).reshape(
            groups_dev, block_len, kv_dev, HD
        )
        value_block = lax.dynamic_slice_in_dim(prefix_value, key_start, block_len, 1).reshape(
            groups_dev, block_len, kv_dev, HD
        )
        scores = (
            jnp.einsum("rkhd,gpkd->rkhgp", queries, key_block, preferred_element_type=jnp.float32)
            * score_scale
        )
        positions = key_start + jnp.arange(block_len, dtype=jnp.int32)
        inside = positions[None, :] < prompt_len[:, None]
        window = (positions[None, :] < SINKS) | (positions[None, :] >= row_low[:, None])
        usable = member[:, :, None] & inside[None, :, :] & window[:, None, :]
        usable = usable[:, None, None, :, :]
        masked = jnp.where(usable, scores, FAR_BELOW)
        updated = jnp.maximum(running, jnp.max(masked, axis=(3, 4)))
        weights = jnp.where(usable, jnp.exp(masked - updated[..., None, None]), 0.0)
        rescale = jnp.exp(running - updated)
        weight_sum = weight_sum * rescale + jnp.sum(weights, axis=(3, 4))
        rounded = weights.astype(jnp.bfloat16)
        weighted = weighted * rescale[..., None] + jnp.einsum(
            "rkhgp,gpkd->rkhd", rounded, value_block, preferred_element_type=jnp.float32
        )
        return (updated, weight_sum, weighted)

    initial = (
        jnp.full((row_count, kv_dev, repeat), FAR_BELOW, jnp.float32),
        jnp.zeros((row_count, kv_dev, repeat), jnp.float32),
        jnp.zeros((row_count, kv_dev, repeat, HD), jnp.float32),
    )
    running, weight_sum, weighted = lax.fori_loop(0, blocks, key_step, initial)
    bounded = jnp.maximum(weight_sum, 1.0)
    normalized = jnp.where(owned[:, None, None, None], weighted / bounded[..., None], 0.0).reshape(
        row_count, heads_dev * HD
    )
    log_total = jnp.where(owned[:, None, None], running + jnp.log(bounded), 0.0).reshape(
        row_count, heads_dev
    )
    return (normalized, log_total)


def body(
    query,
    new_key,
    new_value,
    prefix_key,
    prefix_value,
    suffix_key,
    suffix_value,
    group_ids,
    prompt_len,
    suffix_len,
    o_weight,
    residual,
    norm_gain,
):
    req_dev = query.shape[0]
    heads_dev = query.shape[1] // HD
    kv_dev = new_key.shape[1] // HD
    repeat = heads_dev // kv_dev
    groups_dev = prefix_key.shape[0]
    prompt_max = prefix_key.shape[1]
    suffix_max = suffix_key.shape[1]
    block_len = min(512, prompt_max)
    score_scale = 1.0 / math.sqrt(HD)
    places = lax.axis_size("req")
    device = lax.axis_index("req")
    first_group = device * groups_dev
    own_suffix = lax.dynamic_slice_in_dim(suffix_len, device * req_dev, req_dev)
    blocks = prompt_max // block_len
    capacity = max(2, req_dev // places)
    slot_total = places * capacity
    all_groups = group_ids.reshape(places, 1, req_dev)
    all_suffix = suffix_len.reshape(places, 1, req_dev)
    all_rows = (
        jnp.arange(places, dtype=jnp.int32)[:, None] * req_dev
        + jnp.arange(req_dev, dtype=jnp.int32)[None, :]
    ).reshape(places, 1, req_dev)
    is_mine = (group_ids // groups_dev).reshape(places, req_dev) == device
    slot_order = jnp.cumsum(is_mine.astype(jnp.int32), axis=1) - 1
    slot_pick = is_mine[:, None, :] & (
        slot_order[:, None, :] == jnp.arange(capacity, dtype=jnp.int32)[None, :, None]
    )
    filled = jnp.any(slot_pick, axis=2)
    slot_group = jnp.where(
        filled, jnp.sum(jnp.where(slot_pick, all_groups, 0), axis=2), -1
    ).reshape(slot_total)
    slot_suffix = jnp.sum(jnp.where(slot_pick, all_suffix, 0), axis=2).reshape(slot_total)
    slot_row = jnp.where(filled, jnp.sum(jnp.where(slot_pick, all_rows, 0), axis=2), -1).reshape(
        slot_total
    )
    every_query = lax.all_gather(query, "req", axis=0, tiled=True)
    pick_rows = slot_row[:, None] == jnp.arange(places * req_dev, dtype=jnp.int32)[None, :]
    compact = jnp.dot(
        pick_rows.astype(jnp.bfloat16), every_query, preferred_element_type=jnp.float32
    ).astype(jnp.bfloat16)
    part_out, part_log = prefix_attend(
        compact, slot_group, slot_suffix, prefix_key, prefix_value, prompt_len, first_group, blocks
    )
    spread_rows = pick_rows.T.astype(jnp.float32)
    spread_out = jnp.dot(spread_rows, part_out, precision=lax.Precision.HIGHEST)
    spread_log = jnp.dot(spread_rows, part_log, precision=lax.Precision.HIGHEST)
    prefix_out, prefix_log = (
        lax.psum_scatter(spread_out, "req", scatter_dimension=0, tiled=True),
        lax.psum_scatter(spread_log, "req", scatter_dimension=0, tiled=True),
    )
    queries = query.reshape(req_dev, kv_dev, repeat, HD)
    key_rows = suffix_key.reshape(req_dev, suffix_max, kv_dev, HD)
    value_rows = suffix_value.reshape(req_dev, suffix_max, kv_dev, HD)
    scores = (
        jnp.einsum("rkhd,rjkd->rkhj", queries, key_rows, preferred_element_type=jnp.float32)
        * score_scale
    )
    own_score = (
        jnp.einsum(
            "rkhd,rkd->rkh",
            queries,
            new_key.reshape(req_dev, kv_dev, HD),
            preferred_element_type=jnp.float32,
        )
        * score_scale
    )
    usable = (jnp.arange(suffix_max, dtype=jnp.int32)[None, :] < own_suffix[:, None])[
        :, None, None, :
    ]
    masked = jnp.where(usable, scores, FAR_BELOW)
    running = jnp.maximum(jnp.max(masked, axis=-1), own_score)
    weights = jnp.where(usable, jnp.exp(masked - running[..., None]), 0.0)
    own_weight = jnp.exp(own_score - running)
    weight_sum = jnp.sum(weights, axis=-1) + own_weight
    weighted = jnp.einsum(
        "rkhj,rjkd->rkhd",
        weights.astype(jnp.bfloat16),
        value_rows,
        preferred_element_type=jnp.float32,
    )
    own_rounded = own_weight.astype(jnp.bfloat16).astype(jnp.float32)
    weighted = weighted + own_rounded[..., None] * new_value.reshape(req_dev, kv_dev, 1, HD).astype(
        jnp.float32
    )
    local_out = weighted / weight_sum[..., None]
    local_log = running + jnp.log(weight_sum)
    prefix_out = prefix_out.reshape(req_dev, kv_dev, repeat, HD)
    prefix_log = prefix_log.reshape(req_dev, kv_dev, repeat)
    combined = jnp.logaddexp(prefix_log, local_log)
    attended = (
        prefix_out * jnp.exp(prefix_log - combined)[..., None]
        + local_out * jnp.exp(local_log - combined)[..., None]
    )
    attended = attended.reshape(req_dev, heads_dev * HD).astype(jnp.bfloat16)
    partial_value = jnp.dot(attended, o_weight, preferred_element_type=jnp.float32)
    proj = lax.psum(partial_value, "tp")
    summed = residual.astype(jnp.float32) + proj
    hidden = summed.astype(jnp.bfloat16)
    inverse = lax.rsqrt(jnp.mean(summed * summed, axis=-1, keepdims=True) + NORM_EPS)
    normed = (summed * inverse * norm_gain.astype(jnp.float32)[None, :]).astype(jnp.bfloat16)
    return (hidden, normed)


def solution(mesh):
    placed = (
        P("req", "tp"),
        P("req", "tp"),
        P("req", "tp"),
        P("req", None, "tp"),
        P("req", None, "tp"),
        P("req", None, "tp"),
        P("req", None, "tp"),
        P(),
        P("req"),
        P(),
        P("tp", None),
        P("req", None),
        P(),
    )
    return jax.shard_map(
        body,
        mesh=mesh,
        in_specs=placed,
        out_specs=(P("req", None), P("req", None)),
        check_vma=False,
    )
```

profile of v0, /device:TPU:2, one launch (start us, length us, event | category | flops | bytes accessed | tf_op | source)
XLA Modules:
  0.0 305.6 jit_solution(10688126659396240701)
XLA Ops:
  11.4 24.9 %all_gather.3 = bf16[768,512]{1,0:T(8,128)(2,1)S(1)} all-gather(bf16[24,512]{1,0:T(8,128)(2,1)} %param.15), channel_id=1, replica_groups=mesh['req'=32,'tp'=8] {'req'}, dimensions={0}, use_global_device_ids=true | all-gather | bytes 811008 | tf_op jit(solution)/shard_map/all_gather | solution.py:127
  36.8 50.0 %while.18 = (s32[]{:T(128)}, f32[64,1,4]{0,2,1:T(4,128)S(1)}, f32[64,1,4]{0,2,1:T(4,128)S(1)}, f32[64,1,4,128]{3,0,2,1:T(8,128)S(1)}, s32[2]{0:T(128)}, /*index=...) while((s32[]{:T(128)}, f32[64,1,4]{0,2,1:T(4,128)S(1)}, ...), condition=%wide.region_9.10_spmd.clone, body=%wide.region_6.9_spmd.clone.sunk | while | flops 136876160 | bytes 4351967 | solution.py:66
  37.8 1.4 fusion.83
  39.6 1.4 fusion.86
  42.0 1.4 fusion.83
  43.8 1.4 fusion.86
  47.9 1.4 fusion.86
  52.1 1.4 fusion.86
  56.3 1.4 fusion.86
  58.7 1.4 fusion.83
  60.5 1.4 fusion.86
  62.9 1.4 fusion.83
  64.6 1.4 fusion.86
  68.8 1.4 fusion.86
  73.0 1.4 fusion.86
  77.1 1.4 fusion.86
  81.3 1.4 fusion.86
  83.7 1.4 fusion.83
  85.5 1.4 fusion.86
  87.2 2.0 fusion.27
  91.6 109.0 %all-reduce = f32[768,4]{0,1:T(4,128)S(1)} all-reduce(f32[768,4]{0,1:T(4,128)S(1)} %fusion.26), channel_id=3, replica_groups=mesh['req'=32,'tp'=8] {'req'}, use_global_device_ids=true, to_apply=%region_11.12.clone | all-reduce | flops 3072 | bytes 24576
  203.2 3.6 %fusion.37 = f32[24,4096]{1,0:T(8,128)} fusion(bf16[512,4096]{1,0:T(8,128)(2,1)} %param.25, bf16[3,8,4,128]{3,2,1,0:T(4,128)(2,1)S(1)} %bitcast.93), kind=kOutput, calls=%fused_computation.57 | convolution fusion | flops 100663296 | bytes 4612096 | tf_op jit(solution)/shard_map/dot_general | solution.py:186
  206.8 88.9 %all-reduce.3.cloned.1.call-done = f32[24,4096]{1,0:T(8,128)} async-done(((f32[24,4096]{1,0:T(8,128)}), f32[24,4096]{1,0:T(8,128)}) %all-reduce.3.cloned.1.call-update) | async-done | bytes 393232 | tf_op jit(solution)/shard_map/psum | solution.py:187
  297.0 1.8 multiply_convert_fusion
  (201 shorter events, 35.8 us)
Async XLA Ops:
  7.2 193.8 %copy-start = (bf16[24,128,128]{2,1,0:T(8,128)(2,1)S(1)}, bf16[24,128,128]{2,1,0:T(8,128)(2,1)}, u32[]{:S(2)}) copy-start(bf16[24,128,128]{2,1,0:T(8,128)(2,1)} %param.20) | copy-start | bytes 2359300
  7.2 194.8 %reduce-scatter.3.cloned.1.call-start = ((), (), s32[]{:S(2)}) async-start(), calls=%async_computation.1 | async-start | bytes 1622016 | tf_op jit(solution)/shard_map/reduce_scatter | solution.py:139
  86.9 2.4 copy-start.2
  86.9 3.2 %copy-start.7 = (u32[256]{0:T(256)S(1)}, u32[256]{0:T(256)}, u32[]{:S(2)}) copy-start(u32[256]{0:T(256)} %constant.130) | copy-start | bytes 3076
  86.9 113.9 %copy-start.4 = (bf16[24,128]{1,0:T(8,128)(2,1)S(1)}, bf16[24,128]{1,0:T(8,128)(2,1)}, u32[]{:S(2)}) copy-start(bf16[24,128]{1,0:T(8,128)(2,1)} %param.17) | copy-start | bytes 18436
  86.9 113.9 %copy-start.6 = (bf16[24,128]{1,0:T(8,128)(2,1)S(1)}, bf16[24,128]{1,0:T(8,128)(2,1)}, u32[]{:S(2)}) copy-start(bf16[24,128]{1,0:T(8,128)(2,1)} %param.16) | copy-start | bytes 18436
  86.9 115.8 %copy-start.5 = (bf16[24,128,128]{2,1,0:T(8,128)(2,1)S(1)}, bf16[24,128,128]{2,1,0:T(8,128)(2,1)}, u32[]{:S(2)}) copy-start(bf16[24,128,128]{2,1,0:T(8,128)(2,1)} %param.21) | copy-start | bytes 2359300
  89.2 206.5 %all-reduce.3.cloned.1.call-start = ((), (), s32[]{:S(2)}) async-start(), calls=%async_computation.2 | async-start | bytes 786432 | tf_op jit(solution)/shard_map/psum | solution.py:187
  202.8 4.0 %copy-start.3 = (bf16[4096]{0:T(1024)(128)(2,1)S(1)}, bf16[4096]{0:T(1024)(128)(2,1)}, u32[]{:S(2)}) copy-start(bf16[4096]{0:T(1024)(128)(2,1)} %param.27) | copy-start | bytes 24580
  202.8 93.0 %copy-start.1 = (bf16[24,4096]{1,0:T(8,128)(2,1)S(1)}, bf16[24,4096]{1,0:T(8,128)(2,1)}, u32[]{:S(2)}) copy-start(bf16[24,4096]{1,0:T(8,128)(2,1)} %param.26) | copy-start | bytes 589828
Sparse Core Ops, SparseCore 0:
  89.4 86.8 reduce-scatter.2
  206.9 88.8 all-reduce.2
where the time goes:
time: 307 us; the launch traced here: 306 us
  blocking collectives  134 us (44%)
  waiting for transfers between devices  89 us (29%)
  matrix products  40.4 us (13%)
  other arithmetic  21.3 us (7%)
  between operations  15 us (5%)
  local copies, waits for them, and re-layouts  5.04 us (2%)
    unnamed x1, blocking collectives  109 us
    psum x1, waiting for transfers between devices, body(): proj = lax.psum(partial_value, 'tp')  88.9 us
    all_gather x1, blocking collectives, body(): every_query = lax.all_gather(query, 'req', axis=0, tiled=True)  24.9 us
    dot_general x12, matrix products, key_step(): jnp.einsum('rkhgp,gpkd->rkhd', rounded, value_block, preferred_element_ty...  16.8 us
    dot_general x12, matrix products, key_step(): jnp.einsum('rkhd,gpkd->rkhgp', queries, key_block, preferred_element_type...  16.3 us
    lt x12, other arithmetic, key_step(): inside = positions[None, :] < prompt_len[:, None]  8.77 us
  transfers between devices with their start and end apart: 2, of which 1 were waited for; matrix products, arithmetic and copies ran while one was open for 1% of the time, Pallas kernels for 0%

commit v1 on v0

--- a/solution.py
+++ b/solution.py
@@ -1,3 +1,4 @@
+import functools
 import math
 import jax
 import jax.numpy as jnp
@@ -9,6 +10,18 @@
 SINKS = 4
 FAR_BELOW = -1e30
 NORM_EPS = 1e-06
+
+
+def domain_spread(s0, net_axis):
+    cores_n = lax.axis_size(net_axis)
+    chunks = [cores_n if kk == 0 else 1 for kk in range(s0.ndim)]
+    piece_now = lax.all_to_all(
+        jnp.tile(s0, chunks), net_axis, split_axis=0, concat_axis=0, tiled=True
+    )
+    return piece_now
+
+
+divide_waves_in = functools.partial(domain_spread, net_axis="req")
 
 
 def prefix_attend(
@@ -124,7 +137,7 @@
     slot_row = jnp.where(filled, jnp.sum(jnp.where(slot_pick, all_rows, 0), axis=2), -1).reshape(
         slot_total
     )
-    every_query = lax.all_gather(query, "req", axis=0, tiled=True)
+    every_query = divide_waves_in(query)
     pick_rows = slot_row[:, None] == jnp.arange(places * req_dev, dtype=jnp.int32)[None, :]
     compact = jnp.dot(
         pick_rows.astype(jnp.bfloat16), every_query, preferred_element_type=jnp.float32

time: 307 us -> 292 us (0.951)
  blocking collectives: 134 us -> 110 us
  other arithmetic: 21.3 us -> 13.3 us
  waiting for transfers between devices: 89 us -> 96.8 us
  starting transfers between devices: 0.08 us -> 7.7 us
    all_gather x1 -> x0, blocking collectives: 24.9 us -> none  [body(): every_query = lax.all_gather(query, 'req', axis=0, tiled=True)]
    lt x12, other arithmetic: 8.77 us -> 0.89 us  [key_step(): inside = positions[None, :] < prompt_len[:, None]]
    all_to_all x0 -> x1, waiting for transfers between devices: none -> 7.68 us  [domain_spread(): lax.all_to_all(jnp.tile(s0, chunks), net_axis, split_axis=0, concat_axis=...]
    all_to_all x0 -> x1, starting transfers between devices: none -> 7.62 us  [domain_spread(): lax.all_to_all(jnp.tile(s0, chunks), net_axis, split_axis=0, concat_axis=...]
  transfers between devices with their start and end apart: 2 -> 3, of which waited for: 1 -> 2; matrix products, arithmetic and copies ran while one was open for 1% -> 2% of each run, Pallas kernels for 0% -> 0%
where the time goes in v1:
time: 292 us; the launch traced here: 291 us
  blocking collectives  110 us (38%)
  waiting for transfers between devices  96.8 us (33%)
  matrix products  40.4 us (14%)
  between operations  15 us (5%)
  other arithmetic  13.3 us (5%)
  starting transfers between devices  7.7 us (3%)
  local copies, waits for them, and re-layouts  6.8 us (2%)
    unnamed x1, blocking collectives  110 us
    psum x1, waiting for transfers between devices, body(): proj = lax.psum(partial_value, 'tp')  89.1 us
    dot_general x12, matrix products, key_step(): jnp.einsum('rkhgp,gpkd->rkhd', rounded, value_block, preferred_element_ty...  16.8 us
    dot_general x12, matrix products, key_step(): jnp.einsum('rkhd,gpkd->rkhgp', queries, key_block, preferred_element_type...  16.3 us
    all_to_all x1, waiting for transfers between devices, domain_spread(): lax.all_to_all(jnp.tile(s0, chunks), net_axis, split_axis=0, concat_axis=...  7.68 us
    all_to_all x1, starting transfers between devices, domain_spread(): lax.all_to_all(jnp.tile(s0, chunks), net_axis, split_axis=0, concat_axis=...  7.62 us
  transfers between devices with their start and end apart: 3, of which 2 were waited for; matrix products, arithmetic and copies ran while one was open for 2% of the time, Pallas kernels for 0%

profile of v1, /device:TPU:2, one launch (start us, length us, event | category | flops | bytes accessed | tf_op | source)
XLA Modules:
  0.0 290.8 jit_solution(12943070124509745079)
XLA Ops:
  7.2 1.7 tile.2
  8.9 7.6 %all-to-all-start = ((bf16[32,24,512]{2,1,0:T(8,128)(2,1)}), bf16[32,24,512]{2,1,0:T(8,128)(2,1)S(1)}, u32[]{:S(2)}, u32[]{:S(2)}) async-start(bf16[32,24,512]{2,1,0:T(8,128)(2,1)} %tile.2), calls=%async_computation | async-start | bytes 1572864 | tf_op jit(solution)/shard_map/all_to_all | solution.py:18
  20.9 7.7 %all-to-all-done = bf16[32,24,512]{2,1,0:T(8,128)(2,1)S(1)} async-done(((bf16[32,24,512]{2,1,0:T(8,128)(2,1)}), bf16[32,24,512]{2,1,0:T(8,128)(2,1)S(1)}, u32[]{:S(2)}, u32[]{:S(2)}) %all-to-all-start) | async-done | bytes 786464 | tf_op jit(solution)/shard_map/all_to_all | solution.py:18
  29.0 42.2 %while.18 = (s32[]{:T(128)}, f32[64,1,4]{0,2,1:T(4,128)S(1)}, f32[64,1,4]{0,2,1:T(4,128)S(1)}, f32[64,1,4,128]{3,0,2,1:T(8,128)S(1)}, s32[2]{0:T(128)S(1)}, /*in...) while((s32[]{:T(128)}, f32[64,1,4]{0,2,1:T(4,128)S(1)}, ...), condition=%wide.region_9.10_spmd.clone, body=%wide.region_6.9_spmd.clone.sunk | while | flops 136876160 | bytes 4351967 | solution.py:79
  31.1 1.4 fusion.86
  34.6 1.4 fusion.86
  38.1 1.4 fusion.86
  39.9 1.4 fusion.83
  41.6 1.4 fusion.86
  45.1 1.4 fusion.86
  48.7 1.4 fusion.86
  50.4 1.4 fusion.83
  52.2 1.4 fusion.86
  55.7 1.4 fusion.86
  59.2 1.4 fusion.86
  60.9 1.4 fusion.83
  62.7 1.4 fusion.86
  66.2 1.4 fusion.86
  69.7 1.4 fusion.86
  71.4 2.0 fusion.27
  76.9 109.8 %all-reduce = f32[768,4]{0,1:T(4,128)S(1)} all-reduce(f32[768,4]{0,1:T(4,128)S(1)} %fusion.26), channel_id=3, replica_groups=mesh['req'=32,'tp'=8] {'req'}, use_global_device_ids=true, to_apply=%region_11.12.clone | all-reduce | flops 3072 | bytes 24576
  188.2 3.6 %fusion.37 = f32[24,4096]{1,0:T(8,128)} fusion(bf16[512,4096]{1,0:T(8,128)(2,1)} %param.25, bf16[3,8,4,128]{3,2,1,0:T(4,128)(2,1)S(1)} %bitcast.95), kind=kOutput, calls=%fused_computation.57 | convolution fusion | flops 100663296 | bytes 4612096 | tf_op jit(solution)/shard_map/dot_general | solution.py:199
  191.9 89.1 %all-reduce.3.cloned.1.call-done = f32[24,4096]{1,0:T(8,128)} async-done(((f32[24,4096]{1,0:T(8,128)}), f32[24,4096]{1,0:T(8,128)}) %all-reduce.3.cloned.1.call-update) | async-done | bytes 393232 | tf_op jit(solution)/shard_map/psum | solution.py:200
  282.1 1.8 multiply_convert_fusion
  (205 shorter events, 30.6 us)
Async XLA Ops:
  7.2 68.7 %copy-start = (bf16[24,128,128]{2,1,0:T(8,128)(2,1)S(1)}, bf16[24,128,128]{2,1,0:T(8,128)(2,1)}, u32[]{:S(2)}) copy-start(bf16[24,128,128]{2,1,0:T(8,128)(2,1)} %param.20) | copy-start | bytes 2359300
  7.2 21.8 %copy-start.3 = (s32[2]{0:T(128)S(1)}, s32[2]{0:T(128)}, u32[]{:S(2)}) copy-start(s32[2]{0:T(128)} %param.23) | copy-start | bytes 28
  8.9 19.7 %all-to-all-start = ((bf16[32,24,512]{2,1,0:T(8,128)(2,1)}), bf16[32,24,512]{2,1,0:T(8,128)(2,1)S(1)}, u32[]{:S(2)}, u32[]{:S(2)}) async-start(bf16[32,24,512]{2,1,0:T(8,128)(2,1)} %tile.2), calls=%async_computation | async-start | bytes 1572864 | tf_op jit(solution)/shard_map/all_to_all | solution.py:18
  16.6 170.4 %reduce-scatter.3.cloned.1.call-start = ((), (), s32[]{:S(2)}) async-start(), calls=%async_computation.2 | async-start | bytes 1622016 | tf_op jit(solution)/shard_map/reduce_scatter | solution.py:152
  71.2 2.4 copy-start.2
  71.2 3.2 %copy-start.5 = (bf16[24,128]{1,0:T(8,128)(2,1)S(1)}, bf16[24,128]{1,0:T(8,128)(2,1)}, u32[]{:S(2)}) copy-start(bf16[24,128]{1,0:T(8,128)(2,1)} %param.17) | copy-start | bytes 18436
  71.2 3.2 %copy-start.8 = (u32[256]{0:T(256)S(1)}, u32[256]{0:T(256)}, u32[]{:S(2)}) copy-start(u32[256]{0:T(256)} %constant.130) | copy-start | bytes 3076
  71.2 4.5 %copy-start.7 = (bf16[24,128]{1,0:T(8,128)(2,1)S(1)}, bf16[24,128]{1,0:T(8,128)(2,1)}, u32[]{:S(2)}) copy-start(bf16[24,128]{1,0:T(8,128)(2,1)} %param.16) | copy-start | bytes 18436
  71.2 116.6 %copy-start.6 = (bf16[24,128,128]{2,1,0:T(8,128)(2,1)S(1)}, bf16[24,128,128]{2,1,0:T(8,128)(2,1)}, u32[]{:S(2)}) copy-start(bf16[24,128,128]{2,1,0:T(8,128)(2,1)} %param.21) | copy-start | bytes 2359300
  73.5 207.4 %all-reduce.3.cloned.1.call-start = ((), (), s32[]{:S(2)}) async-start(), calls=%async_computation.3 | async-start | bytes 786432 | tf_op jit(solution)/shard_map/psum | solution.py:200
  187.8 4.0 %copy-start.4 = (bf16[4096]{0:T(1024)(128)(2,1)S(1)}, bf16[4096]{0:T(1024)(128)(2,1)}, u32[]{:S(2)}) copy-start(bf16[4096]{0:T(1024)(128)(2,1)} %param.27) | copy-start | bytes 24580
  187.8 93.1 %copy-start.1 = (bf16[24,4096]{1,0:T(8,128)(2,1)S(1)}, bf16[24,4096]{1,0:T(8,128)(2,1)}, u32[]{:S(2)}) copy-start(bf16[24,4096]{1,0:T(8,128)(2,1)} %param.26) | copy-start | bytes 589828
Sparse Core Ops, SparseCore 0:
  73.6 87.0 reduce-scatter.2
  192.0 88.9 all-reduce.2
